TPU v7x, 256 devices: a whole 4x4x8 slice. The times are simulated.
256 devices in a mesh: space: 32 (over z_hi, x, core), scen: 8 (over y, z_lo).
Axes of the slice: x: 4, y: 4, z: 8 (z_hi: 4, z_lo: 2; z = z_hi * 2 + z_lo), core: 2. Of those that a mesh axis runs over, the one named last changes fastest.
Arguments:
- concentration: float32 [8, 8, 6, 384, 384], P('scen', None, None, 'space'), may hold values from -6 to 6
- emissions: float32 [8, 6, 384, 384], P('scen', None, 'space'), may hold values from -3 to 3
- courant: float32 [2, 8, 6, 384, 384], P(None, None, None, 'space'), may hold values from -0.9 to 0.9
- tile_source: int32 [8640], P('space'), may hold values from 0 to 215, as said below
- tile_target: int32 [8640], P('space'), may hold values from 0 to 1023, as said below
- intersection: bfloat16 [8640, 128, 128], P('space'), may hold values from 0 to 0.0625
Outputs:
- transported: float32 [8, 8, 6, 384, 384], P('scen', None, None, 'space')
- regridded: float32 [8, 8, 1024, 128], P('scen', None, 'space')
- ensemble_moments: float32 [2, 8, 1024, 128], P(None, None, 'space')
Inputs may be any that keep to these rules, and one draw needn't show every extreme that they name: `tile_source`: every source block of a row band is named by at least one of the band's tiles. `tile_target`: latitude band b holds target blocks b * 32 to (b+1) * 32 - 1. The 270 tiles of one row band name at most 16 blocks of any one latitude band and at least 8 of every latitude band but one, which receives exactly 16 tiles from every row band. Every target block is named by some tile.
All inputs are finite; a program needn't handle non-finite values.
Results may differ from a plain program's by a relative error of at most 0.0027.
Values sent between devices are 32-bit elements; how exact they have to be, the bound alone decides.
No kernel may reach another device: no remote copies, remote signals or barrier semaphores. Data moves between devices by JAX's collectives and lax.ppermute only.
A program may use at most 128 MiB of HBM per device.

v0:
```python
import jax
import jax.numpy as jnp
from jax import lax
from jax.sharding import PartitionSpec as P

TGT_DEV = 32


def broadcast(value, axis, source):
    kept = jnp.where(lax.axis_index(axis) == source, value, 0).astype(value.dtype)
    return lax.psum(kept, axis)


def from_behind(block, axis, distance):
    devices = range(lax.axis_size(axis))
    route = [((i - distance) % len(devices), i) for i in devices]
    return lax.ppermute(block, axis, route)


def parabola_sweep(padded, courant_faces, sweep_axis):
    cells_along = padded.shape[sweep_axis] - 6

    def window(values_in, first_cell, length):
        return lax.slice_in_dim(values_in, first_cell, first_cell + length, axis=sweep_axis)

    edge_values = 7.0 / 12.0 * (
        window(padded, 1, cells_along + 3) + window(padded, 2, cells_along + 3)
    ) - 1.0 / 12.0 * (window(padded, 0, cells_along + 3) + window(padded, 3, cells_along + 3))
    left_edge = window(edge_values, 0, cells_along + 2)
    right_edge = window(edge_values, 1, cells_along + 2)
    centre = window(padded, 2, cells_along + 2)
    slopes = right_edge - left_edge
    curvature = 6.0 * centre - 3.0 * (left_edge + right_edge)
    backward = -courant_faces
    upwind_left = courant_faces * (
        window(right_edge, 0, cells_along + 1)
        - 0.5
        * courant_faces
        * (
            window(slopes, 0, cells_along + 1)
            - (1.0 - 2.0 * courant_faces / 3.0) * window(curvature, 0, cells_along + 1)
        )
    )
    upwind_right = courant_faces * (
        window(left_edge, 1, cells_along + 1)
        + 0.5
        * backward
        * (
            window(slopes, 1, cells_along + 1)
            + (1.0 - 2.0 * backward / 3.0) * window(curvature, 1, cells_along + 1)
        )
    )
    fluxes = jnp.where(courant_faces >= 0.0, upwind_left, upwind_right)
    return window(padded, 3, cells_along) - (
        window(fluxes, 1, cells_along) - window(fluxes, 0, cells_along)
    )


def pack_rows(tracer, north_wind, lowest):
    row_count = tracer.shape[3]
    width_cells = tracer.shape[4]
    if lowest:
        layers = tracer[:, :, :, 0:3, :]
        wind_row = north_wind[:, :, 0:1, :]
    else:
        layers = tracer[:, :, :, row_count - 3 :, :]
        wind_row = north_wind[:, :, row_count - 1 :, :]
    return jnp.concatenate([layers.reshape(-1, width_cells), wind_row.reshape(-1, width_cells)], 0)


def unpack_rows(packed, tracer_shape):
    split_at = tracer_shape[0] * tracer_shape[1] * 18
    layers = packed[:split_at].reshape(tracer_shape[0], tracer_shape[1], 6, 3, packed.shape[1])
    wind_row = packed[split_at:].reshape(tracer_shape[1], 6, packed.shape[1])
    return (layers, wind_row)


def column_halos(tracer, east_wind, north_wind, position, band_count):
    row_count = tracer.shape[3]
    width_cells = tracer.shape[4]
    received = []
    for root_rank, lowest in ((band_count - 1, False), (0, True)):
        packed = pack_rows(tracer, north_wind, lowest)
        received.append(unpack_rows(broadcast(packed, "space", root_rank), tracer.shape))
    top_layers, top_wind = received[0]
    low_layers, low_wind = received[1]
    start_column = width_cells - (position + 1) * row_count
    padded_faces = []
    speed_faces = []
    for face_number in range(6):
        if face_number % 2 == 0:
            source = lax.dynamic_slice_in_dim(
                top_layers[:, :, (face_number - 2) % 6], start_column, row_count, axis=3
            )
            west_cells = jnp.swapaxes(jnp.flip(source, -1), -1, -2)
            west_speed = jnp.flip(
                lax.dynamic_slice_in_dim(
                    top_wind[:, (face_number - 2) % 6], start_column, row_count, axis=1
                ),
                -1,
            )
            east_cells = tracer[:, :, (face_number + 1) % 6, :, 0:3]
            east_speed = east_wind[:, (face_number + 1) % 6, :, 0]
        else:
            west_cells = tracer[:, :, (face_number - 1) % 6, :, width_cells - 3 :]
            west_speed = east_wind[:, (face_number - 1) % 6, :, width_cells - 1]
            source = lax.dynamic_slice_in_dim(
                low_layers[:, :, (face_number + 2) % 6], start_column, row_count, axis=3
            )
            east_cells = jnp.swapaxes(jnp.flip(source, -1), -1, -2)
            east_speed = jnp.flip(
                lax.dynamic_slice_in_dim(
                    low_wind[:, (face_number + 2) % 6], start_column, row_count, axis=1
                ),
                -1,
            )
        padded_faces.append(
            jnp.concatenate([west_cells, tracer[:, :, face_number], east_cells], -1)
        )
        speeds = jnp.concatenate(
            [west_speed[:, :, None], east_wind[:, face_number], east_speed[:, :, None]], -1
        )
        speed_faces.append(0.5 * (speeds[:, :, :-1] + speeds[:, :, 1:]))
    return (jnp.stack(padded_faces, 2), jnp.stack(speed_faces, 1))


def row_halos(tracer, east_wind, north_wind, position, band_count):
    scenarios = tracer.shape[0]
    levels = tracer.shape[1]
    row_count = tracer.shape[3]
    width_cells = tracer.shape[4]
    shifted = []
    for step_by, lowest in ((-1, True), (1, False)):
        packed = pack_rows(tracer, north_wind, lowest)
        shifted.append(unpack_rows(from_behind(packed, "space", step_by), tracer.shape))
    above_layers, above_wind = shifted[0]
    below_layers, below_wind = shifted[1]
    columns = jnp.concatenate([tracer[..., 0:3], tracer[..., width_cells - 3 :]], -1)
    columns = jnp.swapaxes(columns, -1, -2).reshape(-1, row_count)
    column_speed = jnp.stack([east_wind[..., 0], east_wind[..., width_cells - 1]], -2).reshape(
        -1, row_count
    )
    gathered = lax.all_gather(
        jnp.concatenate([columns, column_speed], 0), "space", axis=1, tiled=True
    )
    split_at = scenarios * levels * 36
    edge_layers = gathered[:split_at].reshape(scenarios, levels, 6, 6, -1)
    edge_speed = gathered[split_at:].reshape(levels, 6, 2, -1)
    at_top = position == band_count - 1
    at_bottom = position == 0
    padded_faces = []
    speed_faces = []
    for face_number in range(6):
        if face_number % 2 == 0:
            north_cells = jnp.where(
                at_top,
                jnp.flip(edge_layers[:, :, (face_number + 2) % 6, 0:3], -1),
                above_layers[:, :, face_number],
            )
            north_speed = jnp.where(
                at_top,
                jnp.flip(edge_speed[:, (face_number + 2) % 6, 0], -1),
                above_wind[:, face_number],
            )
            south_cells = jnp.where(
                at_bottom,
                below_layers[:, :, (face_number - 1) % 6],
                below_layers[:, :, face_number],
            )
            south_speed = jnp.where(
                at_bottom, below_wind[:, (face_number - 1) % 6], below_wind[:, face_number]
            )
        else:
            north_cells = jnp.where(
                at_top, above_layers[:, :, (face_number + 1) % 6], above_layers[:, :, face_number]
            )
            north_speed = jnp.where(
                at_top, above_wind[:, (face_number + 1) % 6], above_wind[:, face_number]
            )
            south_cells = jnp.where(
                at_bottom,
                jnp.flip(edge_layers[:, :, (face_number - 2) % 6, 3:6], -1),
                below_layers[:, :, face_number],
            )
            south_speed = jnp.where(
                at_bottom,
                jnp.flip(edge_speed[:, (face_number - 2) % 6, 1], -1),
                below_wind[:, face_number],
            )
        padded_faces.append(
            jnp.concatenate([south_cells, tracer[:, :, face_number], north_cells], -2)
        )
        speeds = jnp.concatenate(
            [south_speed[:, None, :], north_wind[:, face_number], north_speed[:, None, :]], -2
        )
        speed_faces.append(0.5 * (speeds[:, :-1, :] + speeds[:, 1:, :]))
    return (jnp.stack(padded_faces, 2), jnp.stack(speed_faces, 1))


def local(concentration, emissions, courant, tile_source, tile_target, intersection):
    band_count = lax.axis_size("space")
    position = lax.axis_index("space")
    tracer = concentration.at[:, 0].add(emissions)
    east_wind = courant[0]
    north_wind = courant[1]
    for step_number in range(2):
        padded, courant_faces = column_halos(tracer, east_wind, north_wind, position, band_count)
        tracer = parabola_sweep(padded, courant_faces, 4)
        padded, courant_faces = row_halos(tracer, east_wind, north_wind, position, band_count)
        tracer = parabola_sweep(padded, courant_faces, 3)
    scenarios = tracer.shape[0]
    levels = tracer.shape[1]
    batch_rows = scenarios * levels
    block_cells = intersection.shape[1]
    blocks = tracer.astype(jnp.bfloat16).reshape(batch_rows, -1, block_cells)
    chosen = jnp.take(blocks, tile_source, axis=1)
    partial_value = jnp.einsum(
        "btk,tkc->tbc", chosen, intersection, preferred_element_type=jnp.float32
    )
    inside = (tile_target >= 0) & (tile_target < TGT_DEV * lax.axis_size("space"))
    slot_index = jnp.where(inside, tile_target, TGT_DEV * lax.axis_size("space"))
    empty = jnp.zeros((TGT_DEV * lax.axis_size("space"), batch_rows, block_cells), jnp.float32)
    summed = lax.psum_scatter(
        empty.at[slot_index].add(partial_value, mode="drop"),
        "space",
        scatter_dimension=0,
        tiled=True,
    )
    band_result = jnp.swapaxes(summed, 0, 1)
    regridded = band_result.reshape(scenarios, levels, TGT_DEV, block_cells)
    moment_sums = jnp.stack([jnp.sum(regridded, 0), jnp.sum(regridded * regridded, 0)])
    summed_moments = lax.psum(moment_sums, "scen")
    ensemble_moments = summed_moments / (scenarios * lax.axis_size("scen"))
    return (tracer, regridded, ensemble_moments)


def solution(mesh):
    return jax.shard_map(
        local,
        mesh=mesh,
        in_specs=(
            P("scen", None, None, "space", None),
            P("scen", None, "space", None),
            P(None, None, None, "space", None),
            P("space"),
            P("space"),
            P("space", None, None),
        ),
        out_specs=(
            P("scen", None, None, "space", None),
            P("scen", None, "space", None),
            P(None, None, "space", None),
        ),
        check_vma=False,
    )
```

profile of v0, /device:TPU:2, one launch (start us, length us, event | category | flops | bytes accessed | tf_op | source)
XLA Modules:
  0.0 1000.3 jit_solution(16481117192037455923)
XLA Ops:
  7.2 1.2 copy.3036
  8.4 1.6 slice_bitcast_fusion
  12.5 1.7 fusion.60
  15.7 5.9 copy.2796
  21.6 7.1 fusion.179
  28.7 1.3 fusion.178
  30.0 1.4 slice_bitcast_fusion.74
  31.4 1.9 copy.2633
  34.1 2.6 copy.2637
  36.7 1.4 copy.2636
  38.1 2.6 copy.2641
  41.5 2.6 copy.2645
  44.8 2.6 copy.2649
  48.1 1.2 copy.2653
  53.0 240.5 %all-reduce.10.cloned.1.call-done = (f32[192,384]{1,0:T(8,128)}, f32[192,384]{1,0:T(8,128)}) async-done(((f32[192,384]{1,0:T(8,128)}, f32[192,384]{1,0:T(8,128)}), (f32[192,384]{1,0:T(8,128)}, f32[192,384]{1,0:T(8,128)})) %all-reduce.10.cloned.1.call-update) | async-done | bytes 589840 | tf_op jit(solution)/shard_map/psum | solution.py:11
  296.3 1.5 slice.1216
  304.3 1.7 slice_subtract_fusion.1
  306.0 1.5 reshape.5219
  307.6 1.7 fusion.199
  316.5 1.9 bitcast_dynamic-update-slice_fusion.10
  318.4 1.8 constant_dynamic-update-slice_fusion.4
  320.2 1.8 bitcast_dynamic-update-slice_fusion.9
  327.7 2.7 fusion.17
  333.5 45.6 %all-gather = f32[32,12,384]{2,1,0:T(8,128)S(1)} all-gather(f32[1,12,384]{2,1,0:T(8,128)S(1)} %fusion.150), channel_id=1, replica_groups=mesh['space'=32,'scen'=8] {'space'}, dimensions={0}, use_global_device_ids=true | all-gather | bytes 608256 | tf_op jit(solution)/shard_map/all_gather | solution.py:143
  380.7 2.7 collective-permute-start.1
  385.4 1.4 rev.161
  386.8 1.4 rev.163
  388.2 1.4 rev.165
  390.3 1.4 rev.164
  407.0 275.7 %all-reduce.8.cloned.1.call-done = (f32[192,384]{1,0:T(8,128)}, f32[192,384]{1,0:T(8,128)}) async-done(((f32[192,384]{1,0:T(8,128)}, f32[192,384]{1,0:T(8,128)}), (f32[192,384]{1,0:T(8,128)}, f32[192,384]{1,0:T(8,128)})) %all-reduce.8.cloned.1.call-update) | async-done | bytes 589840 | tf_op jit(solution)/shard_map/psum | solution.py:11
  701.8 1.2 fusion.4
  706.2 45.6 %all-gather.1 = f32[32,12,384]{2,1,0:T(8,128)S(1)} all-gather(f32[1,12,384]{2,1,0:T(8,128)S(1)} %fusion.151), channel_id=1, replica_groups=mesh['space'=32,'scen'=8] {'space'}, dimensions={0}, use_global_device_ids=true | all-gather | bytes 608256 | tf_op jit(solution)/shard_map/all_gather | solution.py:143
  753.1 2.6 collective-permute-start.3
  756.4 1.3 rev.191
  757.8 1.3 rev.192
  759.1 1.3 rev.194
  760.4 1.3 rev.193
  761.7 1.3 rev.195
  763.4 1.4 rev.187
  764.8 1.4 rev.189
  775.8 1.8 gather_fusion
  777.6 4.9 fusion.56
  782.5 2.3 broadcast_in_dim.40
  784.8 27.0 %scatter_fusion = f32[1024,8,128]{2,1,0:T(8,128)} fusion(f32[1024,8,128]{2,1,0:T(8,128)} %broadcast_in_dim.40, s32[270]{0:T(512)S(1)} %copy-done.76, f32[270,8,128]{2,1,0:T(8,128)S(1)} %fusion.56), kind=kCustom, calls=%fused_computation.1 | custom fusion | flops 276480 | bytes 3318840 | tf_op jit(solution)/shard_map/scatter-add | solution.py:224
  811.9 99.2 %reduce-scatter.2.cloned.1.call-done = f32[32,8,128]{2,1,0:T(8,128)} async-done(((f32[1024,8,128]{2,1,0:T(8,128)}), f32[32,8,128]{2,1,0:T(8,128)}) %reduce-scatter.2.cloned.1.call-update) | async-done | bytes 131088 | tf_op jit(solution)/shard_map/reduce_scatter | solution.py:223
  912.1 1.6 pad_maximum_fusion.8
  913.7 1.6 copy.2791
  915.3 76.8 %all-reduce.6.cloned.1.call-done = f32[2,8,32,128]{3,1,2,0:T(8,128)} async-done(((f32[2,8,32,128]{3,1,2,0:T(8,128)}), f32[2,8,32,128]{3,1,2,0:T(8,128)}) %all-reduce.6.cloned.1.call-update) | async-done | bytes 262160 | tf_op jit(solution)/shard_map/psum | solution.py:232
  (534 shorter events, 91.0 us)
Async XLA Ops:
  7.2 286.3 %all-reduce.10.cloned.1.call-start = ((), (), s32[]{:S(2)}) async-start(), calls=%async_computation.4 | async-start | bytes 1179648 | tf_op jit(solution)/shard_map/psum | solution.py:11
  10.0 2.4 copy-start.18
  12.3 2.7 copy-start.20
  14.9 667.8 %all-reduce.8.cloned.1.call-start = ((), (), s32[]{:S(2)}) async-start(), calls=%async_computation.3 | async-start | bytes 1179648 | tf_op jit(solution)/shard_map/psum | solution.py:11
  33.3 266.2 %copy-start.10 = (f32[8,1,12,384]{3,0,2,1:T(8,128)}, f32[8,1,12,384]{3,0,2,1:T(8,128)S(1)}, u32[]{:S(2)}) copy-start(f32[8,1,12,384]{3,0,2,1:T(8,128)S(1)} %copy.2633) | copy-start | bytes 442372
  34.1 265.4 %copy-start.35 = (f32[8,1,12,1]{3,0,2,1:T(8,128)}, f32[8,1,12,1]{3,0,2,1:T(8,128)S(1)}, u32[]{:S(2)}) copy-start(f32[8,1,12,1]{3,0,2,1:T(8,128)S(1)} %copy.2635) | copy-start | bytes 1156
  47.3 2.7 copy-start.74
  47.3 3.2 copy-start.78
  51.9 281.4 %copy-start.69 = (f32[96,12]{0,1:T(8,128)}, f32[96,12]{0,1:T(8,128)S(1)}, u32[]{:S(2)}) copy-start(f32[96,12]{0,1:T(8,128)S(1)} %copy.2662) | copy-start | bytes 13828
  300.4 2.2 copy-start.55
  316.5 5.5 copy-start.7
  316.5 5.5 copy-start.32
  316.5 5.5 copy-start.40
  316.5 6.4 copy-start.5
  316.5 6.4 copy-start.30
  316.5 6.4 copy-start.41
  318.4 6.1 copy-start.3
  318.4 6.1 copy-start.28
  318.4 6.1 copy-start.42
  322.0 4.0 copy-start.1
  322.0 4.0 copy-start.26
  322.0 4.0 copy-start.43
  323.7 4.0 copy-start
  332.7 59.0 %collective-permute-start = (f32[192,384]{1,0:T(8,128)}, f32[192,384]{1,0:T(8,128)}, u32[]{:S(2)}, u32[]{:S(2)}) collective-permute-start(f32[192,384]{1,0:T(8,128)} %pad_maximum_fusion.2), channel_id=1, source_target_pairs={{248,0},{0,8},{8,16},{16,24},{24,32},{32,40},{40,48},{48,56},{56,6... | collective-permute-start | bytes 884744 | tf_op jit(solution)/shard_map/ppermute | solution.py:17
  380.7 12.1 %collective-permute-start.1 = (f32[192,384]{1,0:T(8,128)}, f32[192,384]{1,0:T(8,128)S(1)}, u32[]{:S(2)}, u32[]{:S(2)}) collective-permute-start(f32[192,384]{1,0:T(8,128)} %pad_maximum_fusion.6), channel_id=1, source_target_pairs={{8,0},{16,8},{24,16},{32,24},{40,32},{48,40},{56,48},{64,56},{72,6... | collective-permute-start | bytes 884744 | tf_op jit(solution)/shard_map/ppermute | solution.py:17
  383.9 9.5 copy-start.17
  389.6 4.0 copy-start.16
  406.1 505.1 %reduce-scatter.2.cloned.1.call-start = ((), (), s32[]{:S(2)}) async-start(), calls=%async_computation.1 | async-start | bytes 4325376 | tf_op jit(solution)/shard_map/reduce_scatter | solution.py:223
  406.9 277.1 %copy-start.11 = (f32[8,1,12,384]{3,0,2,1:T(8,128)S(1)}, f32[8,1,12,384]{3,0,2,1:T(8,128)}, u32[]{:S(2)}) copy-start(f32[8,1,12,384]{3,0,2,1:T(8,128)} %copy-done.10) | copy-start | bytes 442372
  406.9 277.1 %copy-start.36 = (f32[8,1,12,1]{3,0,2,1:T(8,128)S(1)}, f32[8,1,12,1]{3,0,2,1:T(8,128)}, u32[]{:S(2)}) copy-start(f32[8,1,12,1]{3,0,2,1:T(8,128)} %copy-done.35) | copy-start | bytes 1156
  682.7 3.9 copy-start.47
  684.0 4.2 copy-start.9
  684.0 4.2 copy-start.34
  685.6 4.2 copy-start.8
  685.6 4.2 copy-start.33
  686.7 4.8 copy-start.6
  686.7 4.8 copy-start.31
  689.0 4.0 copy-start.4
  689.0 4.0 copy-start.29
  690.6 4.0 copy-start.2
  690.6 4.0 copy-start.27
  696.3 2.2 copy-start.58
  705.4 61.8 %collective-permute-start.2 = (f32[192,384]{1,0:T(8,128)}, f32[192,384]{1,0:T(8,128)}, u32[]{:S(2)}, u32[]{:S(2)}) collective-permute-start(f32[192,384]{1,0:T(8,128)} %pad_maximum_fusion), channel_id=1, source_target_pairs={{248,0},{0,8},{8,16},{16,24},{24,32},{32,40},{40,48},{48,56},{56,6... | collective-permute-start | bytes 884744 | tf_op jit(solution)/shard_map/ppermute | solution.py:17
  753.1 15.6 %collective-permute-start.3 = (f32[192,384]{1,0:T(8,128)}, f32[192,384]{1,0:T(8,128)S(1)}, u32[]{:S(2)}, u32[]{:S(2)}) collective-permute-start(f32[192,384]{1,0:T(8,128)} %pad_maximum_fusion.4), channel_id=1, source_target_pairs={{8,0},{16,8},{24,16},{32,24},{40,32},{48,40},{56,48},{64,56},{72,6... | collective-permute-start | bytes 884744 | tf_op jit(solution)/shard_map/ppermute | solution.py:17
  769.9 2.5 copy-start.45
  774.7 2.9 copy-start.77
  782.5 2.3 copy-start.76
  811.9 180.2 %all-reduce.6.cloned.1.call-start = ((), (), s32[]{:S(2)}) async-start(), calls=%async_computation.2 | async-start | bytes 524288 | tf_op jit(solution)/shard_map/psum | solution.py:232
  (39 other events, 49.5 us)
Sparse Core Ops, SparseCore 0:
  15.0 278.3 all-reduce.9
  406.2 276.4 all-reduce.7
  812.0 99.1 reduce-scatter.1
  914.2 77.8 all-reduce.5
where the time goes:
time: 1000 us
  waiting for transfers between devices  692 us (69%)
  local copies, waits for them, and re-layouts  112 us (11%)
  blocking collectives  91.1 us (9%)
  other arithmetic  78.5 us (8%)
  between operations  15.8 us (2%)
    psum x2, waiting for transfers between devices, broadcast(): return lax.psum(kept, axis)  516 us
    reduce_scatter x1, waiting for transfers between devices, local(): lax.psum_scatter(empty.at[slot_index].add(partial_value, mode='drop'), 's...  99.2 us
    all_gather x2, blocking collectives, row_halos(): lax.all_gather(jnp.concatenate([columns, column_speed], 0), 'space', axis...  91.1 us
    psum x1, waiting for transfers between devices, local(): summed_moments = lax.psum(moment_sums, 'scen')  76.8 us
    scatter-add x1, other arithmetic, local(): empty.at[slot_index].add(partial_value, mode='drop')  27 us
    unnamed x62, other arithmetic  21.1 us
    slice x7, local copies, waits for them, and re-layouts, column_halos(): east_wind[:, face_number]  20.5 us
  transfers between devices with their start and end apart: 8, of which 4 were waited for; matrix products, arithmetic and copies ran while one was open for 7% of the time, Pallas kernels for 0%

commit v1 on v0

--- a/solution.py
+++ b/solution.py
@@ -229,7 +229,7 @@
     band_result = jnp.swapaxes(summed, 0, 1)
     regridded = band_result.reshape(scenarios, levels, TGT_DEV, block_cells)
     moment_sums = jnp.stack([jnp.sum(regridded, 0), jnp.sum(regridded * regridded, 0)])
-    summed_moments = lax.psum(moment_sums, "scen")
+    summed_moments = jnp.sum(lax.all_gather(moment_sums, "scen"), axis=0)
     ensemble_moments = summed_moments / (scenarios * lax.axis_size("scen"))
     return (tracer, regridded, ensemble_moments)
 

time: 1000 us -> 979 us (0.979)
  waiting for transfers between devices: 692 us -> 668 us
    psum x1 -> x0, waiting for transfers between devices: 76.8 us -> none  [local(): summed_moments = lax.psum(moment_sums, 'scen')]
    all_gather x0 -> x1, waiting for transfers between devices: none -> 52.9 us  [local(): summed_moments = jnp.sum(lax.all_gather(moment_sums, 'scen'), axis=0)]
where the time goes in v1:
time: 979 us; the launch traced here: 977 us
  waiting for transfers between devices  668 us (68%)
  local copies, waits for them, and re-layouts  112 us (11%)
  blocking collectives  91.1 us (9%)
  other arithmetic  79 us (8%)
  between operations  15.8 us (2%)
    psum x2, waiting for transfers between devices, broadcast(): return lax.psum(kept, axis)  516 us
    reduce_scatter x1, waiting for transfers between devices, local(): lax.psum_scatter(empty.at[slot_index].add(partial_value, mode='drop'), 's...  99.3 us
    all_gather x2, blocking collectives, row_halos(): lax.all_gather(jnp.concatenate([columns, column_speed], 0), 'space', axis...  91.1 us
    all_gather x1, waiting for transfers between devices, local(): summed_moments = jnp.sum(lax.all_gather(moment_sums, 'scen'), axis=0)  52.9 us
    scatter-add x1, other arithmetic, local(): empty.at[slot_index].add(partial_value, mode='drop')  27 us
    unnamed x62, other arithmetic  21.1 us
    slice x7, local copies, waits for them, and re-layouts, column_halos(): east_wind[:, face_number]  20.4 us
  transfers between devices with their start and end apart: 8, of which 4 were waited for; matrix products, arithmetic and copies ran while one was open for 7% of the time, Pallas kernels for 0%

profile of v1, /device:TPU:2, one launch (start us, length us, event | category | flops | bytes accessed | tf_op | source)
XLA Modules:
  0.0 976.8 jit_solution(3458232824893531727)
XLA Ops:
  7.2 1.2 copy.3028
  8.4 1.6 slice_bitcast_fusion
  10.2 1.1 scatter-add.12
  12.5 1.7 fusion.60
  15.7 5.8 copy.2788
  21.5 7.0 fusion.179
  28.6 1.3 fusion.178
  29.9 1.4 slice_bitcast_fusion.74
  31.3 1.9 copy.2622
  34.0 2.6 copy.2626
  36.6 1.4 copy.2625
  38.0 2.6 copy.2630
  41.3 2.6 copy.2634
  44.6 2.6 copy.2638
  47.9 1.2 copy.2642
  52.9 240.6 %all-reduce.7.cloned.1.call-done = (f32[192,384]{1,0:T(8,128)}, f32[192,384]{1,0:T(8,128)}) async-done(((f32[192,384]{1,0:T(8,128)}, f32[192,384]{1,0:T(8,128)}), (f32[192,384]{1,0:T(8,128)}, f32[192,384]{1,0:T(8,128)})) %all-reduce.7.cloned.1.call-update) | async-done | bytes 589840 | tf_op jit(solution)/shard_map/psum | solution.py:11
  296.3 1.5 slice.1216
  304.3 1.7 slice_subtract_fusion.1
  306.0 1.5 reshape.5219
  307.6 1.7 fusion.199
  316.5 1.9 bitcast_dynamic-update-slice_fusion.10
  318.4 1.8 constant_dynamic-update-slice_fusion.4
  320.2 1.8 bitcast_dynamic-update-slice_fusion.9
  327.7 2.7 fusion.17
  333.5 45.6 %all-gather.1 = f32[32,12,384]{2,1,0:T(8,128)S(1)} all-gather(f32[1,12,384]{2,1,0:T(8,128)S(1)} %fusion.150), channel_id=1, replica_groups=mesh['space'=32,'scen'=8] {'space'}, dimensions={0}, use_global_device_ids=true | all-gather | bytes 608256 | tf_op jit(solution)/shard_map/all_gather | solution.py:143
  380.7 2.7 collective-permute-start.1
  385.5 1.4 rev.161
  386.9 1.4 rev.163
  388.3 1.4 rev.165
  390.4 1.4 rev.164
  407.0 275.6 %all-reduce.5.cloned.1.call-done = (f32[192,384]{1,0:T(8,128)}, f32[192,384]{1,0:T(8,128)}) async-done(((f32[192,384]{1,0:T(8,128)}, f32[192,384]{1,0:T(8,128)}), (f32[192,384]{1,0:T(8,128)}, f32[192,384]{1,0:T(8,128)})) %all-reduce.5.cloned.1.call-update) | async-done | bytes 589840 | tf_op jit(solution)/shard_map/psum | solution.py:11
  701.9 1.2 fusion.4
  706.2 45.6 %all-gather.2 = f32[32,12,384]{2,1,0:T(8,128)S(1)} all-gather(f32[1,12,384]{2,1,0:T(8,128)S(1)} %fusion.151), channel_id=1, replica_groups=mesh['space'=32,'scen'=8] {'space'}, dimensions={0}, use_global_device_ids=true | all-gather | bytes 608256 | tf_op jit(solution)/shard_map/all_gather | solution.py:143
  753.2 2.6 collective-permute-start.3
  756.4 1.3 rev.191
  757.8 1.3 rev.192
  759.1 1.3 rev.194
  760.4 1.3 rev.193
  761.7 1.3 rev.195
  763.4 1.4 rev.187
  764.8 1.4 rev.189
  775.8 1.8 gather_fusion
  777.6 4.9 fusion.56
  782.5 2.3 broadcast_in_dim.40
  784.8 27.0 %scatter_fusion = f32[1024,8,128]{2,1,0:T(8,128)} fusion(f32[1024,8,128]{2,1,0:T(8,128)} %broadcast_in_dim.40, s32[270]{0:T(512)S(1)} %copy-done.77, f32[270,8,128]{2,1,0:T(8,128)S(1)} %fusion.56), kind=kCustom, calls=%fused_computation.1 | custom fusion | flops 276480 | bytes 3318840 | tf_op jit(solution)/shard_map/scatter-add | solution.py:224
  812.0 99.3 %reduce-scatter.2.cloned.1.call-done = f32[32,8,128]{2,1,0:T(8,128)} async-done(((f32[1024,8,128]{2,1,0:T(8,128)}), f32[32,8,128]{2,1,0:T(8,128)}) %reduce-scatter.2.cloned.1.call-update) | async-done | bytes 131088 | tf_op jit(solution)/shard_map/reduce_scatter | solution.py:223
  914.7 52.9 %all-gather.5.cloned.1.call-done = f32[16,8,32,128]{3,2,1,0:T(8,128)} async-done(((f32[2,8,32,128]{3,2,1,0:T(8,128)}), f32[16,8,32,128]{3,2,1,0:T(8,128)}) %all-gather.5.cloned.1.call-update) | async-done | bytes 2097168 | tf_op jit(solution)/shard_map/all_gather | solution.py:232
  967.5 1.8 reduce_sum.8
  (538 shorter events, 91.7 us)
Async XLA Ops:
  7.2 286.3 %all-reduce.7.cloned.1.call-start = ((), (), s32[]{:S(2)}) async-start(), calls=%async_computation.4 | async-start | bytes 1179648 | tf_op jit(solution)/shard_map/psum | solution.py:11
  10.0 2.4 copy-start.18
  12.3 2.6 copy-start.20
  14.9 667.8 %all-reduce.5.cloned.1.call-start = ((), (), s32[]{:S(2)}) async-start(), calls=%async_computation.3 | async-start | bytes 1179648 | tf_op jit(solution)/shard_map/psum | solution.py:11
  33.2 266.4 %copy-start.10 = (f32[8,1,12,384]{3,0,2,1:T(8,128)}, f32[8,1,12,384]{3,0,2,1:T(8,128)S(1)}, u32[]{:S(2)}) copy-start(f32[8,1,12,384]{3,0,2,1:T(8,128)S(1)} %copy.2622) | copy-start | bytes 442372
  34.0 265.5 %copy-start.35 = (f32[8,1,12,1]{3,0,2,1:T(8,128)}, f32[8,1,12,1]{3,0,2,1:T(8,128)S(1)}, u32[]{:S(2)}) copy-start(f32[8,1,12,1]{3,0,2,1:T(8,128)S(1)} %copy.2624) | copy-start | bytes 1156
  47.2 2.7 copy-start.75
  47.2 3.3 copy-start.79
  51.9 281.6 %copy-start.70 = (f32[96,12]{0,1:T(8,128)}, f32[96,12]{0,1:T(8,128)S(1)}, u32[]{:S(2)}) copy-start(f32[96,12]{0,1:T(8,128)S(1)} %copy.2651) | copy-start | bytes 13828
  300.4 2.2 copy-start.56
  316.5 5.6 copy-start.7
  316.5 5.6 copy-start.32
  316.5 5.6 copy-start.41
  316.5 6.4 copy-start.5
  316.5 6.4 copy-start.30
  316.5 6.4 copy-start.42
  318.4 6.2 copy-start.3
  318.4 6.2 copy-start.28
  318.4 6.2 copy-start.43
  322.0 4.1 copy-start.1
  322.0 4.1 copy-start.26
  322.1 4.1 copy-start.44
  323.7 4.1 copy-start
  332.8 59.0 %collective-permute-start = (f32[192,384]{1,0:T(8,128)}, f32[192,384]{1,0:T(8,128)}, u32[]{:S(2)}, u32[]{:S(2)}) collective-permute-start(f32[192,384]{1,0:T(8,128)} %pad_maximum_fusion.2), channel_id=1, source_target_pairs={{248,0},{0,8},{8,16},{16,24},{24,32},{32,40},{40,48},{48,56},{56,6... | collective-permute-start | bytes 884744 | tf_op jit(solution)/shard_map/ppermute | solution.py:17
  380.7 12.0 %collective-permute-start.1 = (f32[192,384]{1,0:T(8,128)}, f32[192,384]{1,0:T(8,128)S(1)}, u32[]{:S(2)}, u32[]{:S(2)}) collective-permute-start(f32[192,384]{1,0:T(8,128)} %pad_maximum_fusion.6), channel_id=1, source_target_pairs={{8,0},{16,8},{24,16},{32,24},{40,32},{48,40},{56,48},{64,56},{72,6... | collective-permute-start | bytes 884744 | tf_op jit(solution)/shard_map/ppermute | solution.py:17
  384.0 9.5 copy-start.17
  389.7 4.0 copy-start.16
  406.1 505.1 %reduce-scatter.2.cloned.1.call-start = ((), (), s32[]{:S(2)}) async-start(), calls=%async_computation.1 | async-start | bytes 4325376 | tf_op jit(solution)/shard_map/reduce_scatter | solution.py:223
  407.0 277.0 %copy-start.11 = (f32[8,1,12,384]{3,0,2,1:T(8,128)S(1)}, f32[8,1,12,384]{3,0,2,1:T(8,128)}, u32[]{:S(2)}) copy-start(f32[8,1,12,384]{3,0,2,1:T(8,128)} %copy-done.10) | copy-start | bytes 442372
  407.0 277.0 %copy-start.36 = (f32[8,1,12,1]{3,0,2,1:T(8,128)S(1)}, f32[8,1,12,1]{3,0,2,1:T(8,128)}, u32[]{:S(2)}) copy-start(f32[8,1,12,1]{3,0,2,1:T(8,128)} %copy-done.35) | copy-start | bytes 1156
  682.7 3.9 copy-start.48
  684.0 4.2 copy-start.9
  684.0 4.2 copy-start.34
  685.6 4.2 copy-start.8
  685.6 4.2 copy-start.33
  686.6 4.8 copy-start.6
  686.6 4.8 copy-start.31
  689.0 4.0 copy-start.4
  689.0 4.0 copy-start.29
  690.6 4.0 copy-start.2
  690.6 4.0 copy-start.27
  705.5 61.8 %collective-permute-start.2 = (f32[192,384]{1,0:T(8,128)}, f32[192,384]{1,0:T(8,128)}, u32[]{:S(2)}, u32[]{:S(2)}) collective-permute-start(f32[192,384]{1,0:T(8,128)} %pad_maximum_fusion), channel_id=1, source_target_pairs={{248,0},{0,8},{8,16},{16,24},{24,32},{32,40},{40,48},{48,56},{56,6... | collective-permute-start | bytes 884744 | tf_op jit(solution)/shard_map/ppermute | solution.py:17
  753.2 15.6 %collective-permute-start.3 = (f32[192,384]{1,0:T(8,128)}, f32[192,384]{1,0:T(8,128)S(1)}, u32[]{:S(2)}, u32[]{:S(2)}) collective-permute-start(f32[192,384]{1,0:T(8,128)} %pad_maximum_fusion.4), channel_id=1, source_target_pairs={{8,0},{16,8},{24,16},{32,24},{40,32},{48,40},{56,48},{64,56},{72,6... | collective-permute-start | bytes 884744 | tf_op jit(solution)/shard_map/ppermute | solution.py:17
  769.9 2.5 copy-start.46
  774.7 2.9 copy-start.78
  782.5 2.3 copy-start.77
  811.9 155.6 %all-gather.5.cloned.1.call-start = ((), (), s32[]{:S(2)}) async-start(), calls=%async_computation.2 | async-start | bytes 2359296 | tf_op jit(solution)/shard_map/all_gather | solution.py:232
  911.3 2.7 copy-start.37
  (40 other events, 51.6 us)
Sparse Core Ops, SparseCore 0:
  15.0 278.4 all-reduce.6
  406.3 276.3 all-reduce.4
  812.0 99.1 reduce-scatter.1
  914.1 53.3 all-gather.4
